TPU v7x, 512 devices: a whole 4x4x16 slice. The times are simulated.
512 devices in a mesh: seq: 64 (over x, z), tp: 8 (over y, core).
Axes of the slice: x: 4, y: 4, z: 16, core: 2. Of those that a mesh axis runs over, the one named last changes fastest.
Arguments:
- hidden_in: bfloat16 [8192, 2048], P('seq', 'tp'), may hold values from -3 to 3
- norm_gain: float32 [2048], replicated, may hold values from 0.1 to 1.9
- w_query: bfloat16 [2048, 2048], P(None, 'tp'), may hold values from -0.125 to 0.125
- w_key: bfloat16 [2048, 1024], P(None, 'tp'), may hold values from -0.125 to 0.125
- w_value: bfloat16 [2048, 1024], P(None, 'tp'), may hold values from -0.125 to 0.125
- w_headgate: bfloat16 [2048, 16], P(None, 'tp'), may hold values from -0.125 to 0.125
- w_out: bfloat16 [2048, 2048], P('tp'), may hold values from -0.125 to 0.125
- q_gain: float32 [128], replicated, may hold values from 1.5 to 4
- k_gain: float32 [128], replicated, may hold values from 0.1 to 1.9
- cache_keys: bfloat16 [2, 8192, 1024], P(None, 'seq', 'tp'), as said below
- cache_values: bfloat16 [2, 8192, 1024], P(None, 'seq', 'tp'), may hold values from -6 to 6
- cached_len: int32 [8], replicated, may hold values from 0 to 8192, as said below
- group_of: int32 [8], replicated, may hold values from 0 to 1, as said below
Outputs:
- layer_out: bfloat16 [8192, 2048], P('seq', 'tp')
Inputs may be any that keep to these rules, and one draw needn't show every extreme that they name: `cache_keys`: keys of the cached positions, of order one and larger. `cached_len`: some request attends to all 8192 cached positions of its prompt, and some to none. `group_of`: every shared prompt is used by some request.
All inputs are finite; a program needn't handle non-finite values.
Results may differ from a plain program's by a relative error of at most 0.018.
Values may be sent and summed in bfloat16 or wider, within the bound.
No kernel may reach another device: no remote copies, remote signals or barrier semaphores. Data moves between devices by JAX's collectives and lax.ppermute only.
A program may use at most 64 MiB of HBM per device.

v0:
```python
import math
import jax
import jax.numpy as jnp
from jax import lax
from jax.sharding import Mesh, PartitionSpec as P

SPAN = 1024
norm_eps = 1e-06
rope_base = 1000000.0
masked_score = -1e30


def shifted(value, axis, by):
    peers = lax.axis_size(axis)
    pairs = [(i, i + by) for i in range(peers) if 0 <= i + by < peers]
    return lax.ppermute(value, axis, pairs)


def head_norm(vec, gain):
    return vec * lax.rsqrt(jnp.mean(vec * vec, -1, keepdims=True) + norm_eps) * gain


def rotate(vec, positions):
    half = vec.shape[-1] // 2
    freq = jnp.exp(
        jnp.arange(half, dtype=jnp.float32) * (-2.0 * math.log(rope_base) / vec.shape[-1])
    )
    angle = positions.astype(jnp.float32)[:, None] * freq[None, :]
    shape_out = (vec.shape[0],) + (1,) * (vec.ndim - 2) + (half,)
    cosine = jnp.cos(angle).reshape(shape_out)
    sine = jnp.sin(angle).reshape(shape_out)
    first = vec[..., :half]
    second = vec[..., half:]
    return jnp.concatenate([first * cosine - second * sine, second * cosine + first * sine], -1)


def attend(state_now, queries, keys_block, values_block, visible):
    running_max, running_sum, running_acc = state_now
    scores = jnp.einsum(
        "tcgd,kcd->tcgk", queries, keys_block, preferred_element_type=jnp.float32
    ) * queries.shape[-1] ** (-0.5)
    scores = jnp.where(visible[:, None, None, :], scores, masked_score)
    new_max = jnp.maximum(running_max, jnp.max(scores, -1))
    rescale = jnp.exp(running_max - new_max)
    expo = jnp.exp(scores - new_max[..., None])
    new_sum = running_sum * rescale + jnp.sum(expo, -1)
    update = jnp.einsum(
        "tcgk,kcd->tcgd",
        expo.astype(jnp.bfloat16),
        values_block,
        preferred_element_type=jnp.float32,
    )
    return (new_max, new_sum, running_acc * rescale[..., None] + update)


def per_device(
    hidden_in,
    norm_gain,
    w_query,
    w_key,
    w_value,
    w_headgate,
    w_out,
    q_gain,
    k_gain,
    cache_keys,
    cache_values,
    cached_len,
    group_of,
):
    tok_rows = hidden_in.shape[0]
    head_dim = q_gain.shape[0]
    kv_local = w_key.shape[1] // head_dim
    heads_local = w_query.shape[1] // head_dim
    group_size = heads_local // kv_local
    per_request = SPAN // tok_rows
    ring_x = lax.axis_size("sx")
    ring_z = lax.axis_size("sz")
    req_count = ring_x * ring_z // per_request
    pair = ring_z // req_count
    x_index = lax.axis_index("sx")
    z_index = lax.axis_index("sz")
    seq_index = x_index * ring_z + z_index
    request = seq_index % req_count
    local_part = seq_index // req_count
    parity = z_index // req_count
    length = cached_len[request]
    peer_groups = group_of[jnp.arange(ring_z, dtype=jnp.int32) % req_count]
    cache_both = jnp.stack([cache_keys, cache_values], 1)
    incoming = lax.all_to_all(cache_both[peer_groups], "sz", 0, 0, tiled=True)
    cache_rows = ring_z * cache_keys.shape[1]
    keys_cache = incoming[:, 0].reshape(cache_rows, kv_local, head_dim)
    values_cache = incoming[:, 1].reshape(cache_rows, kv_local, head_dim)
    cache_pos = x_index * cache_rows + jnp.arange(cache_rows, dtype=jnp.int32)
    gathered = lax.all_gather(hidden_in, "tp", axis=1, tiled=True)
    widened = gathered.astype(jnp.float32)
    normed = (
        widened * lax.rsqrt(jnp.mean(widened * widened, -1, keepdims=True) + norm_eps) * norm_gain
    ).astype(jnp.bfloat16)
    positions = length + local_part * tok_rows + jnp.arange(tok_rows, dtype=jnp.int32)
    query_raw = jnp.dot(normed, w_query, preferred_element_type=jnp.float32).reshape(
        tok_rows, kv_local, group_size, head_dim
    )
    queries = rotate(head_norm(query_raw, q_gain), positions).astype(jnp.bfloat16)
    key_raw = jnp.dot(normed, w_key, preferred_element_type=jnp.float32).reshape(
        tok_rows, kv_local, head_dim
    )
    keys_new = rotate(head_norm(key_raw, k_gain), positions).astype(jnp.bfloat16)
    values_new = (
        jnp.dot(normed, w_value, preferred_element_type=jnp.float32)
        .astype(jnp.bfloat16)
        .reshape(tok_rows, kv_local, head_dim)
    )
    gates = jax.nn.sigmoid(jnp.dot(normed, w_headgate, preferred_element_type=jnp.float32)).reshape(
        tok_rows, kv_local, group_size
    )
    partner_pairs = [(z, (z + req_count) % ring_z) for z in range(ring_z)]
    partner_keys, partner_values = lax.ppermute((keys_new, values_new), "sz", partner_pairs)
    partner_part = x_index * pair + (pair - 1 - parity)
    all_queries = lax.all_gather(queries, "sx", axis=0, tiled=True)
    query_tok = (
        (jnp.arange(ring_x, dtype=jnp.int32) * pair + parity)[:, None] * tok_rows
        + jnp.arange(tok_rows, dtype=jnp.int32)[None, :]
    ).reshape(-1)
    row_ids = jnp.arange(tok_rows, dtype=jnp.int32)
    key_tok = jnp.concatenate([local_part * tok_rows + row_ids, partner_part * tok_rows + row_ids])
    keys_all = jnp.concatenate([keys_cache, keys_new, partner_keys], 0)
    values_all = jnp.concatenate([values_cache, values_new, partner_values], 0)
    query_count = query_tok.shape[0]
    visible = jnp.concatenate(
        [
            jnp.broadcast_to((cache_pos < length)[None, :], (query_count, cache_rows)),
            key_tok[None, :] <= query_tok[:, None],
        ],
        1,
    )
    scores = jnp.einsum(
        "tcgd,kcd->tcgk", all_queries, keys_all, preferred_element_type=jnp.float32
    ) * head_dim ** (-0.5)
    seen = visible[:, None, None, :]
    scores = jnp.where(seen, scores, masked_score)
    top = jnp.max(scores, -1)
    expo = jnp.where(seen, jnp.exp(scores - top[..., None]), 0.0)
    total = jnp.sum(expo, -1)
    acc = jnp.einsum(
        "tcgk,kcd->tcgd", expo.astype(jnp.bfloat16), values_all, preferred_element_type=jnp.float32
    )
    stats = jnp.stack([top, total], -1).reshape(ring_x, tok_rows, kv_local, group_size, 2)
    acc = acc.reshape(ring_x, tok_rows, kv_local, group_size, head_dim)
    stats_in = lax.all_to_all(stats, "sx", 0, 0, tiled=True)
    acc_in = lax.all_to_all(acc, "sx", 0, 0, tiled=True)
    best = jnp.max(stats_in[..., 0], 0)
    factor = jnp.exp(stats_in[..., 0] - best[None])
    total = jnp.sum(stats_in[..., 1] * factor, 0)
    summed_acc = jnp.sum(acc_in * factor[..., None], 0)
    mixed = (
        (summed_acc / total[..., None] * gates[..., None])
        .astype(jnp.bfloat16)
        .reshape(tok_rows, heads_local * head_dim)
    )
    partial_out = jnp.dot(mixed, w_out, preferred_element_type=jnp.float32)
    tp_size = lax.axis_size("tp")
    pieces = partial_out.astype(jnp.bfloat16).reshape(tok_rows, tp_size, -1)
    arrived = lax.all_to_all(pieces, "tp", 1, 1, tiled=True)
    summed = jnp.sum(arrived.astype(jnp.float32), 1)
    return (hidden_in.astype(jnp.float32) + summed).astype(jnp.bfloat16)


def solution(mesh):
    seq_size = mesh.shape["seq"]
    tp_size = mesh.shape["tp"]
    req_count = seq_size // (SPAN // 128)
    ring_z = 2 * req_count
    ring_x = seq_size // ring_z
    split_mesh = Mesh(mesh.devices.reshape(ring_x, ring_z, tp_size), ("sx", "sz", "tp"))
    seq = ("sx", "sz")
    in_specs = (
        P(seq, "tp"),
        P(),
        P(None, "tp"),
        P(None, "tp"),
        P(None, "tp"),
        P(None, "tp"),
        P("tp", None),
        P(),
        P(),
        P(None, seq, "tp"),
        P(None, seq, "tp"),
        P(),
        P(),
    )
    out_specs = P(seq, "tp")
    return jax.shard_map(
        per_device, mesh=split_mesh, in_specs=in_specs, out_specs=out_specs, check_vma=False
    )
```

profile of v0, /device:TPU:32, one launch (start us, length us, event | category | flops | bytes accessed | tf_op | source)
XLA Modules:
  0.0 155.3 jit_solution(10557558886728345072)
XLA Ops:
  0.0 14.0 %all_gather.6 = bf16[128,2048]{1,0:T(8,128)(2,1)S(1)} all-gather(bf16[128,256]{1,0:T(8,128)(2,1)} %param.13), channel_id=1, replica_groups=mesh['sx'=4,'sz'=16,'tp'=8] {'tp'}, dimensions={1}, use_global_device_ids=true | all-gather | bytes 589824 | tf_op jit(solution)/shard_map/all_gather | solution.py:95
  14.0 0.2 fusion.14
  14.2 2.0 %fusion.10 = bf16[128,1,128]{2,0,1:T(8,128)(2,1)} fusion(bf16[2048,128]{1,0:T(8,128)(2,1)} %param.17, bf16[128,2048]{1,0:T(8,128)(2,1)S(1)} %all_gather.6, f32[2048]{0:T(1024)} %param.14, f32[128]{0:T(128)S(1)} %add_rsqrt_fusion.2), kind=kOutput, calls=%fused_computation.16 | convolution fusion | flops 68173824 | bytes 1090048 | tf_op jit(solution)/shard_map/dot_general | solution.py:110
  16.2 14.8 %collective-permute-start = (bf16[128,1,128]{2,0,1:T(8,128)(2,1)}, bf16[128,1,128]{2,0,1:T(8,128)(2,1)}, u32[]{:S(2)}, u32[]{:S(2)}) collective-permute-start(bf16[128,1,128]{2,0,1:T(8,128)(2,1)} %fusion.10), channel_id=1, source_target_pairs={{0,64},{8,72},{16,80},{24,88},{32,96},{40,104},{48,112},{56,120},{... | collective-permute-start | bytes 98312 | tf_op jit(solution)/shard_map/ppermute | solution.py:118
  31.1 1.3 gather_fusion
  32.4 0.9 pad_maximum_fusion
  33.3 1.7 %gather_fusion.1 = bf16[16,2,128,128]{3,2,1,0:T(8,128)(2,1)} fusion(bf16[2,2,128,128]{3,2,0,1:T(8,128)(2,1)S(1)} %pad_maximum_fusion, s32[1024]{0:T(1024)S(1)} %pad_clamp_fusion), kind=kCustom, calls=%fused_computation.1 | custom fusion | bytes 2097216 | tf_op jit(solution)/shard_map/gather | solution.py:90
  35.0 6.0 %all-to-all-start = ((bf16[16,2,128,128]{3,2,1,0:T(8,128)(2,1)}), bf16[16,2,128,128]{3,2,1,0:T(8,128)(2,1)S(1)}, u32[]{:S(2)}, u32[]{:S(2)}) async-start(bf16[16,2,128,128]{3,2,1,0:T(8,128)(2,1)} %gather_fusion.1), calls=%async_computation | async-start | bytes 2097152 | tf_op jit(solution)/shard_map/all_to_all | solution.py:90
  41.0 1.2 dynamic_slice.3
  42.8 1.5 multiply_reduce_fusion.2
  44.3 0.7 multiply_bitcast_fusion
  45.1 0.2 fusion.33
  45.3 0.6 pad_maximum_fusion.2
  45.9 11.2 %collective-permute-start.1 = (bf16[128,1,128]{0,2,1:T(8,128)(2,1)}, bf16[128,1,128]{0,2,1:T(8,128)(2,1)}, u32[]{:S(2)}, u32[]{:S(2)}) collective-permute-start(bf16[128,1,128]{0,2,1:T(8,128)(2,1)} %pad_maximum_fusion.2), channel_id=1, source_target_pairs={{0,64},{8,72},{16,80},{24,88},{32,96},{40,104},{48,112},{56,120},{... | collective-permute-start | bytes 98312 | tf_op jit(solution)/shard_map/ppermute | solution.py:118
  57.1 1.6 %fusion.49 = f32[128,256]{1,0:T(8,128)S(1)} fusion(bf16[2048,256]{1,0:T(8,128)(2,1)} %param.15, bf16[128,2048]{1,0:T(8,128)(2,1)S(1)} %all_gather.6, f32[2048]{0:T(1024)} %param.14, f32[128]{0:T(128)S(1)} %add_rsqrt_fusion.2), kind=kOutput, calls=%fused_computation.98 | convolution fusion | flops 135266304 | bytes 1712640 | tf_op jit(solution)/shard_map/dot_general | solution.py:101
  58.7 0.1 reshape.449
  58.8 0.2 multiply_reduce_fusion.1
  59.0 0.1 copy.62
  59.1 0.6 add_compare_fusion
  59.7 0.3 multiply_cosine_fusion
  60.1 0.1 fusion.27
  60.2 0.1 subtract_convert_fusion
  60.3 0.1 pad_maximum_fusion.1
  60.4 0.1 add_bitcast_fusion
  60.4 0.1 broadcast_compare_fusion
  60.6 0.3 fusion.13
  60.9 2.2 %pad_add_fusion = pred[512,2304]{0,1:T(8,128)(4,1)S(1)} fusion(pred[512,256]{0,1:T(8,128)(4,1)S(1)} %broadcast_compare_fusion, pred[2304]{0:T(1024)(128)(4,1)S(1)} %pad.9.clone), kind=kLoop, calls=%fused_computation.9 | loop fusion | flops 1179648 | bytes 1313024 | tf_op jit(solution)/shard_map/concatenate | solution.py:130
  63.1 12.6 %all_gather.7 = bf16[512,1,2,128]{3,0,2,1:T(8,128)(2,1)S(1)} all-gather(bf16[128,1,2,128]{3,0,2,1:T(8,128)(2,1)S(1)} %pad_maximum_fusion.1), channel_id=1, replica_groups=mesh['sx'=4,'sz'=16,'tp'=8] {'sx'}, dimensions={0}, use_global_device_ids=true | all-gather | bytes 327680 | tf_op jit(solution)/shard_map/all_gather | solution.py:120
  75.8 1.5 copy.58
  77.2 1.5 copy.60
  78.7 0.0 collective-permute-done
  78.7 1.5 copy.59
  80.1 18.6 %collective-permute-done.1 = bf16[128,1,128]{0,2,1:T(8,128)(2,1)} collective-permute-done((bf16[128,1,128]{0,2,1:T(8,128)(2,1)}, bf16[128,1,128]{0,2,1:T(8,128)(2,1)}, u32[]{:S(2)}, u32[]{:S(2)}) %collective-permute-start.1) | collective-permute-done | bytes 32800 | tf_op jit(solution)/shard_map/ppermute | solution.py:118
  98.7 1.5 copy.61
  100.2 1.1 fusion.54
  101.2 1.2 copy.72
  102.5 6.7 %fusion = (f32[512,2]{0,1:T(2,128)S(1)}, f32[2304,512,2]{1,0,2:T(8,128)}) fusion(pred[512,2304]{0,1:T(8,128)(4,1)S(1)} %pad_add_fusion, bf16[512,1,2,128]{3,0,2,1:T(8,128)(2,1)S(1)} %all_gather.7, bf16[128,1,128]{2,0,1:T(8,128)(2,1)} %copy.61, bf16[128,1,128]{2,0,1:T(8,128)(2,1)} %copy.60, bf16[2048,1,128]{2,0,1:T(8,128)(2,1)} %bitcast.102), kind=kOutput, calls=%fused_computation.4 | convolution fusion | flops 612826112 | bytes 11472896 | tf_op jit(solution)/shard_map/tcgd,kcd->tcgk/dot_general | solution.py:137
  109.3 6.1 %fusion.1 = f32[512,2]{0,1:T(2,128)S(1)} fusion(f32[2304,512,2]{1,0,2:T(8,128)} %get-tuple-element.16, f32[512,2]{0,1:T(2,128)S(1)} %get-tuple-element.15, pred[512,2304]{0,1:T(8,128)(4,1)S(1)} %pad_add_fusion), kind=kLoop, calls=%fused_computation.5 | loop fusion | flops 11795456 | bytes 10625024 | tf_op jit(solution)/shard_map/reduce_sum | solution.py:144
  115.4 0.6 copy.66
  116.0 4.3 %all-to-all-start.2 = ((f32[4,128,1,2,2]{1,3,4,2,0:T(2,128)}), f32[4,128,1,2,2]{1,3,4,2,0:T(2,128)S(1)}, u32[]{:S(2)}, u32[]{:S(2)}) async-start(f32[4,128,1,2,2]{1,3,4,2,0:T(2,128)} %copy.66), calls=%async_computation.2 | async-start | bytes 16384 | tf_op jit(solution)/shard_map/all_to_all | solution.py:150
  120.3 5.1 %fusion.7 = f32[1,2,16,4,8,128]{5,4,3,2,1,0:T(8,128)S(1)} fusion(f32[2304,512,2]{1,0,2:T(8,128)} %get-tuple-element.16, f32[512,2]{0,1:T(2,128)S(1)} %get-tuple-element.15, pred[512,2304]{0,1:T(8,128)(4,1)S(1)} %pad_add_fusion, bf16[128,1,128]{0,2,1:T(8,128)(2,1)S(1)} %copy-done.3, bf16[128,1,128]{0,2,1:T(8,128)(2,1)S(1)} %copy-done.2, ...), kind=kOutput, calls=%fused_computation.14 | convolution fusion | flops 617545728 | bytes 11735040 | tf_op jit(solution)/shard_map/tcgk,kcd->tcgd/dot_general | solution.py:145
  125.4 0.8 copy.84
  126.2 4.8 %all-to-all-start.1 = ((f32[4,128,1,2,128]{1,4,3,2,0:T(8,128)}), f32[4,128,1,2,128]{1,4,3,2,0:T(8,128)S(1)}, u32[]{:S(2)}, u32[]{:S(2)}) async-start(f32[4,128,1,2,128]{1,4,3,2,0:T(8,128)} %bitcast.98), calls=%async_computation.1 | async-start | bytes 1048576 | tf_op jit(solution)/shard_map/all_to_all | solution.py:151
  131.1 9.0 %all-to-all-done.1 = f32[4,128,1,2,128]{1,4,3,2,0:T(8,128)S(1)} async-done(((f32[4,128,1,2,128]{1,4,3,2,0:T(8,128)}), f32[4,128,1,2,128]{1,4,3,2,0:T(8,128)S(1)}, u32[]{:S(2)}, u32[]{:S(2)}) %all-to-all-start.1) | async-done | bytes 524320 | tf_op jit(solution)/shard_map/all_to_all | solution.py:151
  140.2 0.3 convolution_convert_fusion
  140.6 14.0 %all_to_all.20 = bf16[128,8,256]{2,0,1:T(8,128)(2,1)S(1)} all-to-all(bf16[128,8,256]{2,0,1:T(8,128)(2,1)S(1)} %bitcast.100), channel_id=1, replica_groups=mesh['sx'=4,'sz'=16,'tp'=8] {'tp'}, dimensions={1} | all-to-all | bytes 1048576 | tf_op jit(solution)/shard_map/all_to_all | solution.py:164
  154.6 0.1 convert_reduce_fusion
  154.6 0.6 add_convert_fusion
  (38 shorter events, 0.3 us)
Async XLA Ops:
  0.0 140.2 %copy-start = (bf16[256,2048]{1,0:T(8,128)(2,1)S(1)}, bf16[256,2048]{1,0:T(8,128)(2,1)}, u32[]{:S(2)}) copy-start(bf16[256,2048]{1,0:T(8,128)(2,1)} %param.19) | copy-start | bytes 3145732
  0.0 60.6 %copy-start.5 = (f32[2048]{0:T(1024)S(1)}, f32[2048]{0:T(1024)}, u32[]{:S(2)}) copy-start(f32[2048]{0:T(1024)} %param.14) | copy-start | bytes 24580
  0.0 60.0 %copy-start.4 = (f32[128]{0:T(128)S(1)}, f32[128]{0:T(128)}, u32[]{:S(2)}) copy-start(f32[128]{0:T(128)} %param.20) | copy-start | bytes 1540
  0.0 60.6 %copy-start.6 = (bf16[2048,2]{0,1:T(2,128)(2,1)S(1)}, bf16[2048,2]{0,1:T(2,128)(2,1)}, u32[]{:S(2)}) copy-start(bf16[2048,2]{0,1:T(2,128)(2,1)} %param.18) | copy-start | bytes 24580
  16.2 62.4 %collective-permute-start = (bf16[128,1,128]{2,0,1:T(8,128)(2,1)}, bf16[128,1,128]{2,0,1:T(8,128)(2,1)}, u32[]{:S(2)}, u32[]{:S(2)}) collective-permute-start(bf16[128,1,128]{2,0,1:T(8,128)(2,1)} %fusion.10), channel_id=1, source_target_pairs={{0,64},{8,72},{16,80},{24,88},{32,96},{40,104},{48,112},{56,120},{... | collective-permute-start | bytes 98312 | tf_op jit(solution)/shard_map/ppermute | solution.py:118
  35.0 65.2 %all-to-all-start = ((bf16[16,2,128,128]{3,2,1,0:T(8,128)(2,1)}), bf16[16,2,128,128]{3,2,1,0:T(8,128)(2,1)S(1)}, u32[]{:S(2)}, u32[]{:S(2)}) async-start(bf16[16,2,128,128]{3,2,1,0:T(8,128)(2,1)} %gather_fusion.1), calls=%async_computation | async-start | bytes 2097152 | tf_op jit(solution)/shard_map/all_to_all | solution.py:90
  45.9 52.8 %collective-permute-start.1 = (bf16[128,1,128]{0,2,1:T(8,128)(2,1)}, bf16[128,1,128]{0,2,1:T(8,128)(2,1)}, u32[]{:S(2)}, u32[]{:S(2)}) collective-permute-start(bf16[128,1,128]{0,2,1:T(8,128)(2,1)} %pad_maximum_fusion.2), channel_id=1, source_target_pairs={{0,64},{8,72},{16,80},{24,88},{32,96},{40,104},{48,112},{56,120},{... | collective-permute-start | bytes 98312 | tf_op jit(solution)/shard_map/ppermute | solution.py:118
  102.5 17.8 %copy-start.2 = (bf16[128,1,128]{0,2,1:T(8,128)(2,1)S(1)}, bf16[128,1,128]{0,2,1:T(8,128)(2,1)}, u32[]{:S(2)}) copy-start(bf16[128,1,128]{0,2,1:T(8,128)(2,1)} %copy.58) | copy-start | bytes 98308
  102.5 17.8 %copy-start.3 = (bf16[128,1,128]{0,2,1:T(8,128)(2,1)S(1)}, bf16[128,1,128]{0,2,1:T(8,128)(2,1)}, u32[]{:S(2)}) copy-start(bf16[128,1,128]{0,2,1:T(8,128)(2,1)} %copy.59) | copy-start | bytes 98308
  116.0 10.2 %all-to-all-start.2 = ((f32[4,128,1,2,2]{1,3,4,2,0:T(2,128)}), f32[4,128,1,2,2]{1,3,4,2,0:T(2,128)S(1)}, u32[]{:S(2)}, u32[]{:S(2)}) async-start(f32[4,128,1,2,2]{1,3,4,2,0:T(2,128)} %copy.66), calls=%async_computation.2 | async-start | bytes 16384 | tf_op jit(solution)/shard_map/all_to_all | solution.py:150
  120.3 34.3 %copy-start.1 = (bf16[128,256]{1,0:T(8,128)(2,1)S(1)}, bf16[128,256]{1,0:T(8,128)(2,1)}, u32[]{:S(2)}) copy-start(bf16[128,256]{1,0:T(8,128)(2,1)} %param.13) | copy-start | bytes 196612
  126.2 13.9 %all-to-all-start.1 = ((f32[4,128,1,2,128]{1,4,3,2,0:T(8,128)}), f32[4,128,1,2,128]{1,4,3,2,0:T(8,128)S(1)}, u32[]{:S(2)}, u32[]{:S(2)}) async-start(f32[4,128,1,2,128]{1,4,3,2,0:T(8,128)} %bitcast.98), calls=%async_computation.1 | async-start | bytes 1048576 | tf_op jit(solution)/shard_map/all_to_all | solution.py:151
where the time goes:
time: 156 us; the launch traced here: 155 us
  starting transfers between devices  41.1 us (26%)
  blocking collectives  40.6 us (26%)
  waiting for transfers between devices  27.6 us (18%)
  matrix products  17.5 us (11%)
  local copies, waits for them, and re-layouts  14 us (9%)
  other arithmetic  13.5 us (9%)
    ppermute x2, starting transfers between devices, per_device(): lax.ppermute((keys_new, values_new), 'sz', partner_pairs)  26 us
    ppermute x2, waiting for transfers between devices, per_device(): lax.ppermute((keys_new, values_new), 'sz', partner_pairs)  18.6 us
    all_gather x1, blocking collectives, per_device(): gathered = lax.all_gather(hidden_in, 'tp', axis=1, tiled=True)  14 us
    all_to_all x1, blocking collectives, per_device(): arrived = lax.all_to_all(pieces, 'tp', 1, 1, tiled=True)  14 us
    all_gather x1, blocking collectives, per_device(): all_queries = lax.all_gather(queries, 'sx', axis=0, tiled=True)  12.6 us
    all_to_all x1, waiting for transfers between devices, per_device(): acc_in = lax.all_to_all(acc, 'sx', 0, 0, tiled=True)  9.05 us
    dot_general x1, matrix products, per_device(): jnp.einsum('tcgd,kcd->tcgk', all_queries, keys_all, preferred_element_typ...  6.72 us
    reduce_sum x1, other arithmetic, per_device(): total = jnp.sum(expo, -1)  6.14 us
  transfers between devices with their start and end apart: 5, of which 2 were waited for; matrix products, arithmetic and copies ran while one was open for 17% of the time, Pallas kernels for 0%

commit v1 on v0

--- a/solution.py
+++ b/solution.py
@@ -92,7 +92,8 @@
     keys_cache = incoming[:, 0].reshape(cache_rows, kv_local, head_dim)
     values_cache = incoming[:, 1].reshape(cache_rows, kv_local, head_dim)
     cache_pos = x_index * cache_rows + jnp.arange(cache_rows, dtype=jnp.int32)
-    gathered = lax.all_gather(hidden_in, "tp", axis=1, tiled=True)
+    copies = jnp.concatenate([hidden_in] * lax.axis_size("tp"), axis=1)
+    gathered = lax.all_to_all(copies, "tp", 1, 1, tiled=True)
     widened = gathered.astype(jnp.float32)
     normed = (
         widened * lax.rsqrt(jnp.mean(widened * widened, -1, keepdims=True) + norm_eps) * norm_gain

time: 156 us -> 148 us (0.949)
  blocking collectives: 40.6 us -> 27.1 us
  waiting for transfers between devices: 27.6 us -> 33.2 us
  starting transfers between devices: 41.1 us -> 43.3 us
    all_gather x1 -> x0, blocking collectives: 14 us -> none  [per_device(): gathered = lax.all_gather(hidden_in, 'tp', axis=1, tiled=True)]
    ppermute x2, starting transfers between devices: 26 us -> 14.6 us  [per_device(): lax.ppermute((keys_new, values_new), 'sz', partner_pairs)]
    all_to_all x1, starting transfers between devices: 6.04 us -> 15.2 us  [per_device(): incoming = lax.all_to_all(cache_both[peer_groups], 'sz', 0, 0, tiled=True)]
    ppermute x2, waiting for transfers between devices: 18.6 us -> 23.2 us  [per_device(): lax.ppermute((keys_new, values_new), 'sz', partner_pairs)]
    all_to_all x0 -> x1, starting transfers between devices: none -> 4.47 us  [per_device(): gathered = lax.all_to_all(copies, 'tp', 1, 1, tiled=True)]
    all_to_all x0 -> x1, waiting for transfers between devices: none -> 2.03 us  [per_device(): gathered = lax.all_to_all(copies, 'tp', 1, 1, tiled=True)]
  transfers between devices with their start and end apart: 5 -> 6, of which waited for: 2 -> 4; matrix products, arithmetic and copies ran while one was open for 17% -> 16% of each run, Pallas kernels for 0% -> 0%
where the time goes in v1:
time: 148 us
  starting transfers between devices  43.3 us (29%)
  waiting for transfers between devices  33.2 us (22%)
  blocking collectives  27.1 us (18%)
  matrix products  16.7 us (11%)
  local copies, waits for them, and re-layouts  13.5 us (9%)
  other arithmetic  12.7 us (9%)
    ppermute x2, waiting for transfers between devices, per_device(): lax.ppermute((keys_new, values_new), 'sz', partner_pairs)  23.2 us
    all_to_all x1, starting transfers between devices, per_device(): incoming = lax.all_to_all(cache_both[peer_groups], 'sz', 0, 0, tiled=True)  15.2 us
    ppermute x2, starting transfers between devices, per_device(): lax.ppermute((keys_new, values_new), 'sz', partner_pairs)  14.6 us
    all_to_all x1, blocking collectives, per_device(): arrived = lax.all_to_all(pieces, 'tp', 1, 1, tiled=True)  14.5 us
    all_gather x1, blocking collectives, per_device(): all_queries = lax.all_gather(queries, 'sx', axis=0, tiled=True)  12.6 us
    all_to_all x1, waiting for transfers between devices, per_device(): acc_in = lax.all_to_all(acc, 'sx', 0, 0, tiled=True)  8.03 us
    dot_general x1, matrix products, per_device(): jnp.einsum('tcgd,kcd->tcgk', all_queries, keys_all, preferred_element_typ...  6.72 us
    reduce_sum x1, other arithmetic, per_device(): total = jnp.sum(expo, -1)  6.14 us
  transfers between devices with their start and end apart: 6, of which 4 were waited for; matrix products, arithmetic and copies ran while one was open for 16% of the time, Pallas kernels for 0%

profile of v1, /device:TPU:32, one launch (start us, length us, event | category | flops | bytes accessed | tf_op | source)
XLA Modules:
  0.0 147.6 jit_solution(15297850145081769609)
XLA Ops:
  0.0 1.0 copy.68
  1.2 1.0 copy.76
  2.2 4.5 %all-to-all-start.1 = ((bf16[128,8,256]{2,0,1:T(8,128)(2,1)}), bf16[128,8,256]{2,0,1:T(8,128)(2,1)S(1)}, u32[]{:S(2)}, u32[]{:S(2)}) async-start(bf16[128,8,256]{2,0,1:T(8,128)(2,1)} %copy.76), calls=%async_computation.1 | async-start | bytes 1048576 | tf_op jit(solution)/shard_map/all_to_all | solution.py:96
  6.8 1.3 gather_fusion
  8.2 1.2 dynamic_slice.3
  9.4 0.7 add_compare_fusion
  10.1 0.1 broadcast_compare_fusion
  10.2 0.9 pad_maximum_fusion
  11.1 1.7 %gather_fusion.1 = bf16[16,2,128,128]{3,2,1,0:T(8,128)(2,1)} fusion(bf16[2,2,128,128]{3,2,0,1:T(8,128)(2,1)S(1)} %pad_maximum_fusion, s32[1024]{0:T(1024)S(1)} %pad_clamp_fusion), kind=kCustom, calls=%fused_computation.1 | custom fusion | bytes 2097216 | tf_op jit(solution)/shard_map/gather | solution.py:90
  12.8 2.2 %pad_add_fusion = pred[512,2304]{0,1:T(8,128)(4,1)S(1)} fusion(pred[512,256]{0,1:T(8,128)(4,1)S(1)} %broadcast_compare_fusion, pred[2304]{0:T(1024)(128)(4,1)S(1)} %pad.9.clone), kind=kLoop, calls=%fused_computation.9 | loop fusion | flops 1179648 | bytes 1313024 | tf_op jit(solution)/shard_map/concatenate | solution.py:131
  15.0 2.0 %all-to-all-done.1 = bf16[128,8,256]{2,0,1:T(8,128)(2,1)S(1)} async-done(((bf16[128,8,256]{2,0,1:T(8,128)(2,1)}), bf16[128,8,256]{2,0,1:T(8,128)(2,1)S(1)}, u32[]{:S(2)}, u32[]{:S(2)}) %all-to-all-start.1) | async-done | bytes 524320 | tf_op jit(solution)/shard_map/all_to_all | solution.py:96
  17.0 15.2 %all-to-all-start = ((bf16[16,2,128,128]{3,2,1,0:T(8,128)(2,1)}), bf16[16,2,128,128]{3,2,1,0:T(8,128)(2,1)}, u32[]{:S(2)}, u32[]{:S(2)}) async-start(bf16[16,2,128,128]{3,2,1,0:T(8,128)(2,1)} %gather_fusion.1), calls=%async_computation | async-start | bytes 2097152 | tf_op jit(solution)/shard_map/all_to_all | solution.py:90
  32.9 0.3 multiply_cosine_fusion
  33.2 0.3 copy.77
  33.5 0.3 multiply_reduce_fusion
  33.8 0.3 fusion.15
  34.2 1.4 fusion.10
  35.6 11.2 %collective-permute-start = (bf16[128,1,128]{2,0,1:T(8,128)(2,1)S(1)}, bf16[128,1,128]{2,0,1:T(8,128)(2,1)S(1)}, u32[]{:S(2)}, u32[]{:S(2)}) collective-permute-start(bf16[128,1,128]{2,0,1:T(8,128)(2,1)S(1)} %fusion.10), channel_id=1, source_target_pairs={{0,64},{8,72},{16,80},{24,88},{32,96},{40,104},{48,112},{56,120},{... | collective-permute-start | bytes 98312 | tf_op jit(solution)/shard_map/ppermute | solution.py:119
  46.8 1.6 %fusion.48 = f32[128,256]{1,0:T(8,128)S(1)} fusion(bf16[128,2048]{0,1:T(8,128)(2,1)S(1)} %fusion.15, bf16[2048,256]{1,0:T(8,128)(2,1)} %param.15), kind=kOutput, calls=%fused_computation.106 | convolution fusion | flops 134217728 | bytes 1703936 | tf_op jit(solution)/shard_map/dot_general | solution.py:102
  48.4 1.4 multiply_reduce_fusion.3
  49.8 0.1 multiply_bitcast_fusion
  49.9 0.2 fusion.32
  50.1 3.4 %collective-permute-start.1 = (bf16[128,1,128]{0,2,1:T(8,128)(2,1)S(1)}, bf16[128,1,128]{0,2,1:T(8,128)(2,1)S(1)}, u32[]{:S(2)}, u32[]{:S(2)}) collective-permute-start(bf16[128,1,128]{0,2,1:T(8,128)(2,1)S(1)} %pad_maximum_fusion.2), channel_id=1, source_target_pairs={{0,64},{8,72},{16,80},{24,88},{32,96},{40,104},{48,112},{56,120},{... | collective-permute-start | bytes 98312 | tf_op jit(solution)/shard_map/ppermute | solution.py:119
  53.5 0.2 multiply_reduce_fusion.2
  53.8 0.1 fusion.26
  53.9 0.1 subtract_convert_fusion
  54.0 0.1 pad_maximum_fusion.1
  54.1 0.2 fusion.13
  54.3 12.6 %all_gather.3 = bf16[512,1,2,128]{3,0,2,1:T(8,128)(2,1)S(1)} all-gather(bf16[128,1,2,128]{3,0,2,1:T(8,128)(2,1)S(1)} %pad_maximum_fusion.1), channel_id=1, replica_groups=mesh['sx'=4,'sz'=16,'tp'=8] {'sx'}, dimensions={0}, use_global_device_ids=true | all-gather | bytes 327680 | tf_op jit(solution)/shard_map/all_gather | solution.py:121
  66.9 0.7 copy.78
  67.7 0.7 copy.80
  68.4 21.5 %collective-permute-done = bf16[128,1,128]{2,0,1:T(8,128)(2,1)S(1)} collective-permute-done((bf16[128,1,128]{2,0,1:T(8,128)(2,1)S(1)}, bf16[128,1,128]{2,0,1:T(8,128)(2,1)S(1)}, u32[]{:S(2)}, u32[]{:S(2)}) %collective-permute-start) | collective-permute-done | bytes 32800 | tf_op jit(solution)/shard_map/ppermute | solution.py:119
  89.9 0.7 copy.79
  90.6 1.7 %collective-permute-done.1 = bf16[128,1,128]{0,2,1:T(8,128)(2,1)S(1)} collective-permute-done((bf16[128,1,128]{0,2,1:T(8,128)(2,1)S(1)}, bf16[128,1,128]{0,2,1:T(8,128)(2,1)S(1)}, u32[]{:S(2)}, u32[]{:S(2)}) %collective-permute-start.1) | collective-permute-done | bytes 32800 | tf_op jit(solution)/shard_map/ppermute | solution.py:119
  92.2 0.7 copy.81
  93.0 2.1 %fusion.47 = (bf16[16,1,128,128]{3,2,1,0:T(8,128)(2,1)S(1)}, bf16[16,1,128,128]{3,2,1,0:T(8,128)(2,1)}) fusion(bf16[16,2,128,128]{3,2,1,0:T(8,128)(2,1)} %all-to-all-done), kind=kLoop, calls=%fused_computation.105 | loop fusion | bytes 2097152 | tf_op jit(solution)/shard_map/slice | solution.py:93
  95.0 0.2 copy.92
  95.3 6.7 %fusion = (f32[512,2]{0,1:T(2,128)S(1)}, f32[2304,512,2]{1,0,2:T(8,128)}) fusion(pred[512,2304]{0,1:T(8,128)(4,1)S(1)} %pad_add_fusion, bf16[512,1,2,128]{3,0,2,1:T(8,128)(2,1)S(1)} %all_gather.3, bf16[128,1,128]{2,0,1:T(8,128)(2,1)} %copy.81, bf16[128,1,128]{2,0,1:T(8,128)(2,1)} %copy.80, bf16[2048,1,128]{2,0,1:T(8,128)(2,1)} %bitcast.114), kind=kOutput, calls=%fused_computation.4 | convolution fusion | flops 612826112 | bytes 11472896 | tf_op jit(solution)/shard_map/tcgd,kcd->tcgk/dot_general | solution.py:138
  102.0 6.1 %fusion.1 = f32[512,2]{0,1:T(2,128)S(1)} fusion(f32[2304,512,2]{1,0,2:T(8,128)} %get-tuple-element.16, f32[512,2]{0,1:T(2,128)S(1)} %get-tuple-element.15, pred[512,2304]{0,1:T(8,128)(4,1)S(1)} %pad_add_fusion), kind=kLoop, calls=%fused_computation.5 | loop fusion | flops 11795456 | bytes 10625024 | tf_op jit(solution)/shard_map/reduce_sum | solution.py:145
  108.2 0.6 copy.86
  108.8 4.3 %all-to-all-start.3 = ((f32[4,128,1,2,2]{1,3,4,2,0:T(2,128)}), f32[4,128,1,2,2]{1,3,4,2,0:T(2,128)S(1)}, u32[]{:S(2)}, u32[]{:S(2)}) async-start(f32[4,128,1,2,2]{1,3,4,2,0:T(2,128)} %copy.86), calls=%async_computation.3 | async-start | bytes 16384 | tf_op jit(solution)/shard_map/all_to_all | solution.py:151
  113.1 5.1 %fusion.7 = f32[1,2,16,4,8,128]{5,4,3,2,1,0:T(8,128)S(1)} fusion(f32[2304,512,2]{1,0,2:T(8,128)} %get-tuple-element.16, f32[512,2]{0,1:T(2,128)S(1)} %get-tuple-element.15, pred[512,2304]{0,1:T(8,128)(4,1)S(1)} %pad_add_fusion, bf16[128,1,128]{0,2,1:T(8,128)(2,1)S(1)} %copy-done.3, bf16[128,1,128]{0,2,1:T(8,128)(2,1)S(1)} %copy-done.2, ...), kind=kOutput, calls=%fused_computation.12 | convolution fusion | flops 617545728 | bytes 11735040 | tf_op jit(solution)/shard_map/tcgk,kcd->tcgd/dot_general | solution.py:146
  118.2 0.8 copy.104
  119.0 4.8 %all-to-all-start.2 = ((f32[4,128,1,2,128]{1,4,3,2,0:T(8,128)}), f32[4,128,1,2,128]{1,4,3,2,0:T(8,128)S(1)}, u32[]{:S(2)}, u32[]{:S(2)}) async-start(f32[4,128,1,2,128]{1,4,3,2,0:T(8,128)} %bitcast.109), calls=%async_computation.2 | async-start | bytes 1048576 | tf_op jit(solution)/shard_map/all_to_all | solution.py:152
  123.9 8.0 %all-to-all-done.2 = f32[4,128,1,2,128]{1,4,3,2,0:T(8,128)S(1)} async-done(((f32[4,128,1,2,128]{1,4,3,2,0:T(8,128)}), f32[4,128,1,2,128]{1,4,3,2,0:T(8,128)S(1)}, u32[]{:S(2)}, u32[]{:S(2)}) %all-to-all-start.2) | async-done | bytes 524320 | tf_op jit(solution)/shard_map/all_to_all | solution.py:152
  132.0 0.3 convolution_convert_fusion
  132.4 14.5 %all_to_all.29 = bf16[128,8,256]{2,0,1:T(8,128)(2,1)S(1)} all-to-all(bf16[128,8,256]{2,0,1:T(8,128)(2,1)S(1)} %bitcast.111), channel_id=1, replica_groups=mesh['sx'=4,'sz'=16,'tp'=8] {'tp'}, dimensions={1} | all-to-all | bytes 1048576 | tf_op jit(solution)/shard_map/all_to_all | solution.py:165
  146.9 0.6 add_convert_fusion
  (53 shorter events, 0.7 us)
Async XLA Ops:
  0.0 132.0 %copy-start = (bf16[256,2048]{1,0:T(8,128)(2,1)S(1)}, bf16[256,2048]{1,0:T(8,128)(2,1)}, u32[]{:S(2)}) copy-start(bf16[256,2048]{1,0:T(8,128)(2,1)} %param.19) | copy-start | bytes 3145732
  0.0 33.8 %copy-start.4 = (f32[2048]{0:T(1024)S(1)}, f32[2048]{0:T(1024)}, u32[]{:S(2)}) copy-start(f32[2048]{0:T(1024)} %param.14) | copy-start | bytes 24580
  0.0 49.8 %copy-start.6 = (f32[128]{0:T(128)S(1)}, f32[128]{0:T(128)}, u32[]{:S(2)}) copy-start(f32[128]{0:T(128)} %param.21) | copy-start | bytes 1540
  0.0 53.8 %copy-start.7 = (f32[128]{0:T(128)S(1)}, f32[128]{0:T(128)}, u32[]{:S(2)}) copy-start(f32[128]{0:T(128)} %param.20) | copy-start | bytes 1540
  0.0 54.1 %copy-start.5 = (bf16[2048,2]{0,1:T(2,128)(2,1)S(1)}, bf16[2048,2]{0,1:T(2,128)(2,1)}, u32[]{:S(2)}) copy-start(bf16[2048,2]{0,1:T(2,128)(2,1)} %param.18) | copy-start | bytes 24580
  2.2 14.8 %all-to-all-start.1 = ((bf16[128,8,256]{2,0,1:T(8,128)(2,1)}), bf16[128,8,256]{2,0,1:T(8,128)(2,1)S(1)}, u32[]{:S(2)}, u32[]{:S(2)}) async-start(bf16[128,8,256]{2,0,1:T(8,128)(2,1)} %copy.76), calls=%async_computation.1 | async-start | bytes 1048576 | tf_op jit(solution)/shard_map/all_to_all | solution.py:96
  17.0 75.9 %all-to-all-start = ((bf16[16,2,128,128]{3,2,1,0:T(8,128)(2,1)}), bf16[16,2,128,128]{3,2,1,0:T(8,128)(2,1)}, u32[]{:S(2)}, u32[]{:S(2)}) async-start(bf16[16,2,128,128]{3,2,1,0:T(8,128)(2,1)} %gather_fusion.1), calls=%async_computation | async-start | bytes 2097152 | tf_op jit(solution)/shard_map/all_to_all | solution.py:90
  35.6 54.3 %collective-permute-start = (bf16[128,1,128]{2,0,1:T(8,128)(2,1)S(1)}, bf16[128,1,128]{2,0,1:T(8,128)(2,1)S(1)}, u32[]{:S(2)}, u32[]{:S(2)}) collective-permute-start(bf16[128,1,128]{2,0,1:T(8,128)(2,1)S(1)} %fusion.10), channel_id=1, source_target_pairs={{0,64},{8,72},{16,80},{24,88},{32,96},{40,104},{48,112},{56,120},{... | collective-permute-start | bytes 98312 | tf_op jit(solution)/shard_map/ppermute | solution.py:119
  50.1 42.1 %collective-permute-start.1 = (bf16[128,1,128]{0,2,1:T(8,128)(2,1)S(1)}, bf16[128,1,128]{0,2,1:T(8,128)(2,1)S(1)}, u32[]{:S(2)}, u32[]{:S(2)}) collective-permute-start(bf16[128,1,128]{0,2,1:T(8,128)(2,1)S(1)} %pad_maximum_fusion.2), channel_id=1, source_target_pairs={{0,64},{8,72},{16,80},{24,88},{32,96},{40,104},{48,112},{56,120},{... | collective-permute-start | bytes 98312 | tf_op jit(solution)/shard_map/ppermute | solution.py:119
  95.3 17.8 %copy-start.2 = (bf16[128,1,128]{0,2,1:T(8,128)(2,1)S(1)}, bf16[128,1,128]{0,2,1:T(8,128)(2,1)}, u32[]{:S(2)}) copy-start(bf16[128,1,128]{0,2,1:T(8,128)(2,1)} %copy.78) | copy-start | bytes 98308
  95.3 17.8 %copy-start.3 = (bf16[128,1,128]{0,2,1:T(8,128)(2,1)S(1)}, bf16[128,1,128]{0,2,1:T(8,128)(2,1)}, u32[]{:S(2)}) copy-start(bf16[128,1,128]{0,2,1:T(8,128)(2,1)} %copy.79) | copy-start | bytes 98308
  108.8 10.2 %all-to-all-start.3 = ((f32[4,128,1,2,2]{1,3,4,2,0:T(2,128)}), f32[4,128,1,2,2]{1,3,4,2,0:T(2,128)S(1)}, u32[]{:S(2)}, u32[]{:S(2)}) async-start(f32[4,128,1,2,2]{1,3,4,2,0:T(2,128)} %copy.86), calls=%async_computation.3 | async-start | bytes 16384 | tf_op jit(solution)/shard_map/all_to_all | solution.py:151
  113.1 33.8 %copy-start.1 = (bf16[128,256]{1,0:T(8,128)(2,1)S(1)}, bf16[128,256]{1,0:T(8,128)(2,1)}, u32[]{:S(2)}) copy-start(bf16[128,256]{1,0:T(8,128)(2,1)} %param.13) | copy-start | bytes 196612
  119.0 12.9 %all-to-all-start.2 = ((f32[4,128,1,2,128]{1,4,3,2,0:T(8,128)}), f32[4,128,1,2,128]{1,4,3,2,0:T(8,128)S(1)}, u32[]{:S(2)}, u32[]{:S(2)}) async-start(f32[4,128,1,2,128]{1,4,3,2,0:T(8,128)} %bitcast.109), calls=%async_computation.2 | async-start | bytes 1048576 | tf_op jit(solution)/shard_map/all_to_all | solution.py:152
